TPU v7x, 512 devices: a whole 4x4x16 slice. The times are simulated.
512 devices in a mesh: vox: 32 (over y, x, core), tm: 16 (over z).
Axes of the slice: x: 4, y: 4, z: 16, core: 2. Of those that a mesh axis runs over, the one named last changes fastest.
Arguments:
- series: float32 [2048, 65536], P('tm', 'vox'), may hold values from -40 to 40
- spikes: int32 [2048, 65536], P('tm', 'vox'), may hold values from 0 to 15
- motion: float32 [2048, 6], P('tm'), may hold values from -5 to 5
- tissue: float32 [3, 65536], P(None, 'vox'), may hold values from 0.01 to 12, as said below
Outputs:
- cleaned: float32 [2048, 65536], P('tm', 'vox')
Inputs may be any that keep to these rules, and one draw needn't show every extreme that they name: Bit j-1 of an entry (spikes // 2^(j-1) odd) flags that frame's level-j coefficient of that voxel as a spike. `tissue`: all weights are positive.
All inputs are finite; a program needn't handle non-finite values.
Results may differ from a plain program's by a relative error of at most 0.0003.
Values sent between devices are 32-bit elements; how exact they have to be, the bound alone decides.
No kernel may reach another device: no remote copies, remote signals or barrier semaphores. Data moves between devices by JAX's collectives and lax.ppermute only.
A program may use at most 64 MiB of HBM per device.

v0:
```python
import jax
import jax.numpy as jnp
from jax import lax
from jax.sharding import PartitionSpec as P

LEVELS = 4


def from_behind(block, axis, distance):
    devices = range(lax.axis_size(axis))
    route = [((i - distance) % len(devices), i) for i in devices]
    return lax.ppermute(block, axis, route)


def shifted(block, axis, distance):
    devices = range(lax.axis_size(axis))
    route = [(i - distance, i) for i in devices if i - distance in devices]
    return lax.ppermute(block, axis, route)


def precise_product(left, right):
    return jnp.dot(left, right, precision=lax.Precision.HIGHEST, preferred_element_type=jnp.float32)


def keep_level(spikes, level):
    return 1.0 - (spikes // 2**level % 2).astype(jnp.float32)


def despike_levelwise(series, spikes):
    frames = series.shape[0]
    approx = series
    kept_list = []
    for level in range(LEVELS):
        shift_rows = 2**level
        earlier = from_behind(approx[frames - shift_rows :], "tm", 1)
        lagged = jnp.concatenate([earlier, approx[: frames - shift_rows]], axis=0)
        detail = (approx - lagged) * 0.5
        kept_list.append(detail * keep_level(spikes, level))
        approx = (approx + lagged) * 0.5
    for level in range(LEVELS - 1, -1, -1):
        shift_rows = 2**level
        kept = kept_list[level]
        heads = from_behind(jnp.stack([approx[:shift_rows], kept[:shift_rows]]), "tm", -1)
        lead_approx = jnp.concatenate([approx[shift_rows:], heads[0]], axis=0)
        lead_kept = jnp.concatenate([kept[shift_rows:], heads[1]], axis=0)
        approx = (approx + lead_approx) * 0.5 + (kept - lead_kept) * 0.5
    return approx


def local(series, spikes, motion, tissue):
    spike_free_series = despike_levelwise(series, spikes)
    numer = precise_product(spike_free_series, tissue.T)
    numer = lax.psum(numer, "vox")
    voxel_signals = numer / float(tissue.shape[1] * lax.axis_size("vox"))
    base_regressors = jnp.concatenate([motion, voxel_signals], axis=1)
    previous_frames = shifted(base_regressors[base_regressors.shape[0] - 1 :], "tm", 1)
    before = jnp.concatenate([previous_frames, base_regressors[:-1]], axis=0)
    temporal_derivative = base_regressors - before
    nuisance_matrix = jnp.concatenate(
        [
            base_regressors,
            temporal_derivative,
            base_regressors * base_regressors,
            temporal_derivative * temporal_derivative,
        ],
        axis=1,
    )
    gram_matrix = precise_product(nuisance_matrix.T, nuisance_matrix)
    cross_products = precise_product(nuisance_matrix.T, spike_free_series)
    gram_matrix, cross_products = lax.psum((gram_matrix, cross_products), "tm")
    factor = jnp.linalg.cholesky(gram_matrix)
    beta_estimates = jax.scipy.linalg.cho_solve((factor, True), cross_products)
    return spike_free_series - precise_product(nuisance_matrix, beta_estimates)


def solution(mesh):
    return jax.shard_map(
        local,
        mesh=mesh,
        in_specs=(P("tm", "vox"), P("tm", "vox"), P("tm", None), P(None, "vox")),
        out_specs=P("tm", "vox"),
        check_vma=False,
    )
```

profile of v0, /device:TPU:2, one launch (start us, length us, event | category | flops | bytes accessed | tf_op | source)
XLA Modules:
  0.0 347.5 jit_solution(11441887220270911308)
XLA Ops:
  6.5 0.9 slice.120
  7.4 3.8 %collective-permute-start = (f32[1,2048]{1,0:T(1,128)S(1)}, f32[1,2048]{1,0:T(1,128)S(1)}, u32[]{:S(2)}, u32[]{:S(2)}) collective-permute-start(f32[1,2048]{1,0:T(1,128)S(1)} %slice.120), channel_id=1, source_target_pairs={{15,0},{0,1},{1,2},{2,3},{3,4},{4,5},{5,6},{6,7},{7,8},{8,9},{9,10... | collective-permute-start | bytes 24584 | tf_op jit(solution)/shard_map/ppermute | solution.py:12
  11.2 9.2 %collective-permute-done = f32[1,2048]{1,0:T(1,128)S(1)} collective-permute-done((f32[1,2048]{1,0:T(1,128)S(1)}, f32[1,2048]{1,0:T(1,128)S(1)}, u32[]{:S(2)}, u32[]{:S(2)}) %collective-permute-start) | collective-permute-done | bytes 8224 | tf_op jit(solution)/shard_map/ppermute | solution.py:12
  20.4 2.6 fusion.16
  23.1 1.9 collective-permute-start.1
  25.0 4.9 %collective-permute-done.1 = f32[2,2048]{1,0:T(2,128)S(1)} collective-permute-done((f32[2,2048]{1,0:T(2,128)S(1)}, f32[2,2048]{1,0:T(2,128)S(1)}, u32[]{:S(2)}, u32[]{:S(2)}) %collective-permute-start.1) | collective-permute-done | bytes 16416 | tf_op jit(solution)/shard_map/ppermute | solution.py:12
  29.9 1.3 fusion.13
  31.2 1.9 collective-permute-start.2
  33.1 5.1 %collective-permute-done.2 = f32[4,2048]{1,0:T(4,128)S(1)} collective-permute-done((f32[4,2048]{1,0:T(4,128)S(1)}, f32[4,2048]{1,0:T(4,128)S(1)}, u32[]{:S(2)}, u32[]{:S(2)}) %collective-permute-start.2) | collective-permute-done | bytes 32800 | tf_op jit(solution)/shard_map/ppermute | solution.py:12
  38.2 1.3 fusion.9
  39.5 1.9 collective-permute-start.3
  41.5 5.3 %collective-permute-done.3 = f32[8,2048]{1,0:T(8,128)S(1)} collective-permute-done((f32[8,2048]{1,0:T(8,128)S(1)}, f32[8,2048]{1,0:T(8,128)S(1)}, u32[]{:S(2)}, u32[]{:S(2)}) %collective-permute-start.3) | collective-permute-done | bytes 65568 | tf_op jit(solution)/shard_map/ppermute | solution.py:12
  46.9 1.2 fusion.4
  48.1 1.9 collective-permute-start.4
  50.1 0.1 slice.164
  50.2 5.4 %collective-permute-done.4 = f32[2,8,2048]{2,1,0:T(8,128)S(1)} collective-permute-done((f32[2,8,2048]{2,1,0:T(8,128)S(1)}, f32[2,8,2048]{2,1,0:T(8,128)S(1)}, u32[]{:S(2)}, u32[]{:S(2)}) %collective-permute-start.4) | collective-permute-done | bytes 131104 | tf_op jit(solution)/shard_map/ppermute | solution.py:12
  55.7 0.3 fusion.18
  56.1 2.4 collective-permute-start.5
  58.5 0.1 slice.170
  58.6 0.1 slice.166
  58.7 3.5 %collective-permute-done.5 = f32[2,4,2048]{2,1,0:T(4,128)S(1)} collective-permute-done((f32[2,4,2048]{2,1,0:T(4,128)S(1)}, f32[2,4,2048]{2,1,0:T(4,128)S(1)}, u32[]{:S(2)}, u32[]{:S(2)}) %collective-permute-start.5) | collective-permute-done | bytes 65568 | tf_op jit(solution)/shard_map/ppermute | solution.py:12
  62.2 0.3 fusion.20
  62.6 4.0 %collective-permute-start.6 = (f32[2,2,2048]{2,1,0:T(2,128)S(1)}, f32[2,2,2048]{2,1,0:T(2,128)S(1)}, u32[]{:S(2)}, u32[]{:S(2)}) collective-permute-start(f32[2,2,2048]{2,1,0:T(2,128)S(1)} %pad_maximum_fusion.6), channel_id=1, source_target_pairs={{1,0},{2,1},{3,2},{4,3},{5,4},{6,5},{7,6},{8,7},{9,8},{10,9},{11,1... | collective-permute-start | bytes 98312 | tf_op jit(solution)/shard_map/ppermute | solution.py:12
  66.6 0.1 slice.176
  66.7 0.1 slice.172
  66.8 1.6 collective-permute-done.6
  68.4 0.4 fusion.22
  68.8 5.2 %collective-permute-start.7 = (f32[2,1,2048]{2,1,0:T(1,128)S(1)}, f32[2,1,2048]{2,1,0:T(1,128)S(1)}, u32[]{:S(2)}, u32[]{:S(2)}) collective-permute-start(f32[2,1,2048]{2,1,0:T(1,128)S(1)} %pad_maximum_fusion.7), channel_id=1, source_target_pairs={{1,0},{2,1},{3,2},{4,3},{5,4},{6,5},{7,6},{8,7},{9,8},{10,9},{11,1... | collective-permute-start | bytes 49160 | tf_op jit(solution)/shard_map/ppermute | solution.py:12
  74.1 0.1 slice.178
  74.2 1.2 collective-permute-done.7
  75.5 0.3 fusion.24
  75.8 0.9 fusion.38
  76.7 57.6 %psum.21 = f32[128,3]{0,1:T(4,128)S(1)} all-reduce(f32[128,3]{0,1:T(4,128)S(1)} %fusion.38), channel_id=1, replica_groups=mesh['vox'=32,'tm'=16] {'vox'}, use_global_device_ids=true, to_apply=%region_0.1 | all-reduce | flops 384 | bytes 3072 | tf_op jit(solution)/shard_map/psum | solution.py:53
  134.4 1.3 collective-permute-start.8
  135.7 1.3 collective-permute-done.8
  137.1 0.4 concatenate.60
  137.6 0.2 fusion.39
  137.7 1.4 fusion.40
  139.1 58.9 %psum.22 = f32[36,36]{0,1:T(8,128)S(1)} all-reduce(f32[36,36]{0,1:T(8,128)S(1)} %fusion.39), channel_id=1, replica_groups=mesh['vox'=32,'tm'=16] {'tm'}, use_global_device_ids=true, to_apply=%region_1.2 | all-reduce | flops 1296 | bytes 10368 | tf_op jit(solution)/shard_map/psum | solution.py:70
  198.0 0.1 copy.6
  198.1 3.3 cholesky.16
  201.5 0.7 compare_reduce_fusion
  202.2 0.6 fusion.28
  202.8 2.8 custom-call.10
  205.5 131.3 %all-reduce.2.cloned.1.call-done = f32[36,2048]{1,0:T(8,128)} async-done(((f32[36,2048]{1,0:T(8,128)}), f32[36,2048]{1,0:T(8,128)}) %all-reduce.2.cloned.1.call-update) | async-done | bytes 294928 | tf_op jit(solution)/shard_map/psum | solution.py:70
  336.8 1.4 fusion.31
  338.3 0.4 fusion.29
  338.7 2.0 convolution_subtract_fusion
  (35 shorter events, 0.7 us)
Async XLA Ops:
  6.5 69.2 %copy-start = (f32[3,2048]{1,0:T(4,128)S(1)}, f32[3,2048]{1,0:T(4,128)}, u32[]{:S(2)}) copy-start(f32[3,2048]{1,0:T(4,128)} %param.7) | copy-start | bytes 73732
  6.5 330.3 %all-reduce.2.cloned.1.call-start = ((), (), s32[]{:S(2)}) async-start(), calls=%async_computation | async-start | bytes 655360 | tf_op jit(solution)/shard_map/psum | solution.py:70
  7.4 13.0 %collective-permute-start = (f32[1,2048]{1,0:T(1,128)S(1)}, f32[1,2048]{1,0:T(1,128)S(1)}, u32[]{:S(2)}, u32[]{:S(2)}) collective-permute-start(f32[1,2048]{1,0:T(1,128)S(1)} %slice.120), channel_id=1, source_target_pairs={{15,0},{0,1},{1,2},{2,3},{3,4},{4,5},{5,6},{6,7},{7,8},{8,9},{9,10... | collective-permute-start | bytes 24584 | tf_op jit(solution)/shard_map/ppermute | solution.py:12
  20.4 9.5 %copy-start.1 = (s32[128,2048]{1,0:T(8,128)S(1)}, s32[128,2048]{1,0:T(8,128)}, u32[]{:S(2)}) copy-start(s32[128,2048]{1,0:T(8,128)} %param.5) | copy-start | bytes 3145732
  23.1 6.8 %collective-permute-start.1 = (f32[2,2048]{1,0:T(2,128)S(1)}, f32[2,2048]{1,0:T(2,128)S(1)}, u32[]{:S(2)}, u32[]{:S(2)}) collective-permute-start(f32[2,2048]{1,0:T(2,128)S(1)} %slice.154), channel_id=1, source_target_pairs={{15,0},{0,1},{1,2},{2,3},{3,4},{4,5},{5,6},{6,7},{7,8},{8,9},{9,10... | collective-permute-start | bytes 49160 | tf_op jit(solution)/shard_map/ppermute | solution.py:12
  31.2 7.0 %collective-permute-start.2 = (f32[4,2048]{1,0:T(4,128)S(1)}, f32[4,2048]{1,0:T(4,128)S(1)}, u32[]{:S(2)}, u32[]{:S(2)}) collective-permute-start(f32[4,2048]{1,0:T(4,128)S(1)} %slice.156), channel_id=1, source_target_pairs={{15,0},{0,1},{1,2},{2,3},{3,4},{4,5},{5,6},{6,7},{7,8},{8,9},{9,10... | collective-permute-start | bytes 98312 | tf_op jit(solution)/shard_map/ppermute | solution.py:12
  39.5 7.4 %collective-permute-start.3 = (f32[8,2048]{1,0:T(8,128)S(1)}, f32[8,2048]{1,0:T(8,128)S(1)}, u32[]{:S(2)}, u32[]{:S(2)}) collective-permute-start(f32[8,2048]{1,0:T(8,128)S(1)} %slice.158), channel_id=1, source_target_pairs={{15,0},{0,1},{1,2},{2,3},{3,4},{4,5},{5,6},{6,7},{7,8},{8,9},{9,10... | collective-permute-start | bytes 196616 | tf_op jit(solution)/shard_map/ppermute | solution.py:12
  48.1 7.6 %collective-permute-start.4 = (f32[2,8,2048]{2,1,0:T(8,128)S(1)}, f32[2,8,2048]{2,1,0:T(8,128)S(1)}, u32[]{:S(2)}, u32[]{:S(2)}) collective-permute-start(f32[2,8,2048]{2,1,0:T(8,128)S(1)} %pad_maximum_fusion.4), channel_id=1, source_target_pairs={{1,0},{2,1},{3,2},{4,3},{5,4},{6,5},{7,6},{8,7},{9,8},{10,9},{11,1... | collective-permute-start | bytes 393224 | tf_op jit(solution)/shard_map/ppermute | solution.py:12
  56.1 6.2 %collective-permute-start.5 = (f32[2,4,2048]{2,1,0:T(4,128)S(1)}, f32[2,4,2048]{2,1,0:T(4,128)S(1)}, u32[]{:S(2)}, u32[]{:S(2)}) collective-permute-start(f32[2,4,2048]{2,1,0:T(4,128)S(1)} %pad_maximum_fusion.5), channel_id=1, source_target_pairs={{1,0},{2,1},{3,2},{4,3},{5,4},{6,5},{7,6},{8,7},{9,8},{10,9},{11,1... | collective-permute-start | bytes 196616 | tf_op jit(solution)/shard_map/ppermute | solution.py:12
  62.6 5.8 %collective-permute-start.6 = (f32[2,2,2048]{2,1,0:T(2,128)S(1)}, f32[2,2,2048]{2,1,0:T(2,128)S(1)}, u32[]{:S(2)}, u32[]{:S(2)}) collective-permute-start(f32[2,2,2048]{2,1,0:T(2,128)S(1)} %pad_maximum_fusion.6), channel_id=1, source_target_pairs={{1,0},{2,1},{3,2},{4,3},{5,4},{6,5},{7,6},{8,7},{9,8},{10,9},{11,1... | collective-permute-start | bytes 98312 | tf_op jit(solution)/shard_map/ppermute | solution.py:12
  68.8 6.6 %collective-permute-start.7 = (f32[2,1,2048]{2,1,0:T(1,128)S(1)}, f32[2,1,2048]{2,1,0:T(1,128)S(1)}, u32[]{:S(2)}, u32[]{:S(2)}) collective-permute-start(f32[2,1,2048]{2,1,0:T(1,128)S(1)} %pad_maximum_fusion.7), channel_id=1, source_target_pairs={{1,0},{2,1},{3,2},{4,3},{5,4},{6,5},{7,6},{8,7},{9,8},{10,9},{11,1... | collective-permute-start | bytes 49160 | tf_op jit(solution)/shard_map/ppermute | solution.py:12
  76.7 57.6 %copy-start.2 = (f32[128,6]{0,1:T(8,128)S(1)}, f32[128,6]{0,1:T(8,128)}, u32[]{:S(2)}) copy-start(f32[128,6]{0,1:T(8,128)} %param.6) | copy-start | bytes 9220
  134.4 2.6 collective-permute-start.8
Sparse Core Ops, SparseCore 0:
  201.6 135.1 all-reduce.1
where the time goes:
time: 348 us
  waiting for transfers between devices  169 us (49%)
  blocking collectives  117 us (34%)
  starting transfers between devices  24.4 us (7%)
  other arithmetic  15.3 us (4%)
  between operations  13.7 us (4%)
  matrix products  6.32 us (2%)
    psum x1, waiting for transfers between devices, local(): gram_matrix, cross_products = lax.psum((gram_matrix, cross_products), 'tm')  131 us
    psum x1, blocking collectives, local(): gram_matrix, cross_products = lax.psum((gram_matrix, cross_products), 'tm')  58.9 us
    psum x1, blocking collectives, local(): numer = lax.psum(numer, 'vox')  57.6 us
    ppermute x8, waiting for transfers between devices, from_behind(): return lax.ppermute(block, axis, route)  36.3 us
    ppermute x8, starting transfers between devices, from_behind(): return lax.ppermute(block, axis, route)  23.1 us
  transfers between devices with their start and end apart: 10, of which 10 were waited for; matrix products, arithmetic and copies ran while one was open for 1% of the time, Pallas kernels for 0%

commit v1 on v0

--- a/solution.py
+++ b/solution.py
@@ -50,7 +50,7 @@
 def local(series, spikes, motion, tissue):
     spike_free_series = despike_levelwise(series, spikes)
     numer = precise_product(spike_free_series, tissue.T)
-    numer = lax.psum(numer, "vox")
+    numer = jnp.sum(lax.all_gather(numer, "vox"), axis=0)
     voxel_signals = numer / float(tissue.shape[1] * lax.axis_size("vox"))
     base_regressors = jnp.concatenate([motion, voxel_signals], axis=1)
     previous_frames = shifted(base_regressors[base_regressors.shape[0] - 1 :], "tm", 1)

time: 348 us -> 314 us (0.902)
  blocking collectives: 117 us -> 83.2 us
    psum x1 -> x0, blocking collectives: 57.6 us -> none  [local(): numer = lax.psum(numer, 'vox')]
    all_gather x0 -> x1, blocking collectives: none -> 24.2 us  [local(): numer = jnp.sum(lax.all_gather(numer, 'vox'), axis=0)]
  transfers between devices with their start and end apart: 10 -> 10, of which waited for: 10 -> 10; matrix products, arithmetic and copies ran while one was open for 1% -> 2% of each run, Pallas kernels for 0% -> 0%
where the time goes in v1:
time: 314 us; the launch traced here: 313 us
  waiting for transfers between devices  167 us (53%)
  blocking collectives  83.2 us (26%)
  starting transfers between devices  24.4 us (8%)
  other arithmetic  15.3 us (5%)
  between operations  13.7 us (4%)
  matrix products  6.32 us (2%)
    psum x1, waiting for transfers between devices, local(): gram_matrix, cross_products = lax.psum((gram_matrix, cross_products), 'tm')  130 us
    psum x1, blocking collectives, local(): gram_matrix, cross_products = lax.psum((gram_matrix, cross_products), 'tm')  58.9 us
    ppermute x8, waiting for transfers between devices, from_behind(): return lax.ppermute(block, axis, route)  36.3 us
    all_gather x1, blocking collectives, local(): numer = jnp.sum(lax.all_gather(numer, 'vox'), axis=0)  24.2 us
    ppermute x8, starting transfers between devices, from_behind(): return lax.ppermute(block, axis, route)  23.1 us
    mul x4, other arithmetic, despike_levelwise(): kept_list.append(detail * keep_level(spikes, level))  6.35 us
  transfers between devices with their start and end apart: 10, of which 10 were waited for; matrix products, arithmetic and copies ran while one was open for 2% of the time, Pallas kernels for 0%

profile of v1, /device:TPU:2, one launch (start us, length us, event | category | flops | bytes accessed | tf_op | source)
XLA Modules:
  0.0 313.1 jit_solution(13603526001401679264)
XLA Ops:
  6.5 0.9 slice.120
  7.4 3.8 %collective-permute-start = (f32[1,2048]{1,0:T(1,128)S(1)}, f32[1,2048]{1,0:T(1,128)S(1)}, u32[]{:S(2)}, u32[]{:S(2)}) collective-permute-start(f32[1,2048]{1,0:T(1,128)S(1)} %slice.120), channel_id=1, source_target_pairs={{15,0},{0,1},{1,2},{2,3},{3,4},{4,5},{5,6},{6,7},{7,8},{8,9},{9,10... | collective-permute-start | bytes 24584 | tf_op jit(solution)/shard_map/ppermute | solution.py:12
  11.2 9.2 %collective-permute-done = f32[1,2048]{1,0:T(1,128)S(1)} collective-permute-done((f32[1,2048]{1,0:T(1,128)S(1)}, f32[1,2048]{1,0:T(1,128)S(1)}, u32[]{:S(2)}, u32[]{:S(2)}) %collective-permute-start) | collective-permute-done | bytes 8224 | tf_op jit(solution)/shard_map/ppermute | solution.py:12
  20.4 2.6 fusion.16
  23.1 1.9 collective-permute-start.1
  25.0 4.9 %collective-permute-done.1 = f32[2,2048]{1,0:T(2,128)S(1)} collective-permute-done((f32[2,2048]{1,0:T(2,128)S(1)}, f32[2,2048]{1,0:T(2,128)S(1)}, u32[]{:S(2)}, u32[]{:S(2)}) %collective-permute-start.1) | collective-permute-done | bytes 16416 | tf_op jit(solution)/shard_map/ppermute | solution.py:12
  29.9 1.3 fusion.13
  31.2 1.9 collective-permute-start.2
  33.1 5.1 %collective-permute-done.2 = f32[4,2048]{1,0:T(4,128)S(1)} collective-permute-done((f32[4,2048]{1,0:T(4,128)S(1)}, f32[4,2048]{1,0:T(4,128)S(1)}, u32[]{:S(2)}, u32[]{:S(2)}) %collective-permute-start.2) | collective-permute-done | bytes 32800 | tf_op jit(solution)/shard_map/ppermute | solution.py:12
  38.2 1.3 fusion.9
  39.5 1.9 collective-permute-start.3
  41.5 5.3 %collective-permute-done.3 = f32[8,2048]{1,0:T(8,128)S(1)} collective-permute-done((f32[8,2048]{1,0:T(8,128)S(1)}, f32[8,2048]{1,0:T(8,128)S(1)}, u32[]{:S(2)}, u32[]{:S(2)}) %collective-permute-start.3) | collective-permute-done | bytes 65568 | tf_op jit(solution)/shard_map/ppermute | solution.py:12
  46.9 1.2 fusion.4
  48.1 1.9 collective-permute-start.4
  50.2 5.4 %collective-permute-done.4 = f32[2,8,2048]{2,1,0:T(8,128)S(1)} collective-permute-done((f32[2,8,2048]{2,1,0:T(8,128)S(1)}, f32[2,8,2048]{2,1,0:T(8,128)S(1)}, u32[]{:S(2)}, u32[]{:S(2)}) %collective-permute-start.4) | collective-permute-done | bytes 131104 | tf_op jit(solution)/shard_map/ppermute | solution.py:12
  55.7 0.3 fusion.18
  56.1 2.4 collective-permute-start.5
  58.5 0.1 slice.170
  58.6 0.1 slice.166
  58.7 3.5 %collective-permute-done.5 = f32[2,4,2048]{2,1,0:T(4,128)S(1)} collective-permute-done((f32[2,4,2048]{2,1,0:T(4,128)S(1)}, f32[2,4,2048]{2,1,0:T(4,128)S(1)}, u32[]{:S(2)}, u32[]{:S(2)}) %collective-permute-start.5) | collective-permute-done | bytes 65568 | tf_op jit(solution)/shard_map/ppermute | solution.py:12
  62.2 0.3 fusion.20
  62.6 4.0 %collective-permute-start.6 = (f32[2,2,2048]{2,1,0:T(2,128)S(1)}, f32[2,2,2048]{2,1,0:T(2,128)S(1)}, u32[]{:S(2)}, u32[]{:S(2)}) collective-permute-start(f32[2,2,2048]{2,1,0:T(2,128)S(1)} %pad_maximum_fusion.6), channel_id=1, source_target_pairs={{1,0},{2,1},{3,2},{4,3},{5,4},{6,5},{7,6},{8,7},{9,8},{10,9},{11,1... | collective-permute-start | bytes 98312 | tf_op jit(solution)/shard_map/ppermute | solution.py:12
  66.6 0.1 slice.176
  66.7 0.1 slice.172
  66.8 1.6 collective-permute-done.6
  68.4 0.4 fusion.22
  68.8 5.2 %collective-permute-start.7 = (f32[2,1,2048]{2,1,0:T(1,128)S(1)}, f32[2,1,2048]{2,1,0:T(1,128)S(1)}, u32[]{:S(2)}, u32[]{:S(2)}) collective-permute-start(f32[2,1,2048]{2,1,0:T(1,128)S(1)} %pad_maximum_fusion.7), channel_id=1, source_target_pairs={{1,0},{2,1},{3,2},{4,3},{5,4},{6,5},{7,6},{8,7},{9,8},{10,9},{11,1... | collective-permute-start | bytes 49160 | tf_op jit(solution)/shard_map/ppermute | solution.py:12
  74.1 0.1 slice.178
  74.2 1.2 collective-permute-done.7
  75.5 0.3 fusion.24
  75.8 0.9 fusion.38
  76.7 24.2 %all-gather = f32[4096,3]{0,1:T(4,128)S(1)} all-gather(f32[128,3]{0,1:T(4,128)S(1)} %fusion.38), channel_id=2, replica_groups=mesh['vox'=32,'tm'=16] {'vox'}, dimensions={0}, use_global_device_ids=true | all-gather | bytes 50688 | tf_op jit(solution)/shard_map/all_gather | solution.py:53
  101.0 0.7 copy-done.2
  101.7 1.3 collective-permute-start.8
  103.0 1.3 collective-permute-done.8
  104.5 0.4 concatenate.60
  104.9 0.2 fusion.39
  105.1 1.4 fusion.40
  106.4 58.9 %psum.14 = f32[36,36]{0,1:T(8,128)S(1)} all-reduce(f32[36,36]{0,1:T(8,128)S(1)} %fusion.39), channel_id=1, replica_groups=mesh['vox'=32,'tm'=16] {'tm'}, use_global_device_ids=true, to_apply=%region_1.2 | all-reduce | flops 1296 | bytes 10368 | tf_op jit(solution)/shard_map/psum | solution.py:70
  165.4 0.1 copy.6
  165.5 3.3 %cholesky.16 = f32[36,36]{1,0:T(8,128)S(1)} custom-call(f32[36,36]{1,0:T(8,128)S(1)} %fusion.33), custom_call_target="Cholesky" | custom-call | tf_op jit(solution)/shard_map/jit(cholesky)/cholesky | solution.py:71
  168.8 0.7 compare_reduce_fusion
  169.5 0.6 fusion.28
  170.1 2.8 custom-call.10
  172.8 129.5 %all-reduce.2.cloned.1.call-done = f32[36,2048]{1,0:T(8,128)} async-done(((f32[36,2048]{1,0:T(8,128)}), f32[36,2048]{1,0:T(8,128)}) %all-reduce.2.cloned.1.call-update) | async-done | bytes 294928 | tf_op jit(solution)/shard_map/psum | solution.py:70
  302.4 1.4 fusion.31
  303.8 0.4 fusion.29
  304.3 2.0 convolution_subtract_fusion
  (36 shorter events, 0.8 us)
Async XLA Ops:
  6.5 69.2 %copy-start = (f32[3,2048]{1,0:T(4,128)S(1)}, f32[3,2048]{1,0:T(4,128)}, u32[]{:S(2)}) copy-start(f32[3,2048]{1,0:T(4,128)} %param.7) | copy-start | bytes 73732
  6.5 295.9 %all-reduce.2.cloned.1.call-start = ((), (), s32[]{:S(2)}) async-start(), calls=%async_computation | async-start | bytes 655360 | tf_op jit(solution)/shard_map/psum | solution.py:70
  7.4 13.0 %collective-permute-start = (f32[1,2048]{1,0:T(1,128)S(1)}, f32[1,2048]{1,0:T(1,128)S(1)}, u32[]{:S(2)}, u32[]{:S(2)}) collective-permute-start(f32[1,2048]{1,0:T(1,128)S(1)} %slice.120), channel_id=1, source_target_pairs={{15,0},{0,1},{1,2},{2,3},{3,4},{4,5},{5,6},{6,7},{7,8},{8,9},{9,10... | collective-permute-start | bytes 24584 | tf_op jit(solution)/shard_map/ppermute | solution.py:12
  20.4 9.5 %copy-start.1 = (s32[128,2048]{1,0:T(8,128)S(1)}, s32[128,2048]{1,0:T(8,128)}, u32[]{:S(2)}) copy-start(s32[128,2048]{1,0:T(8,128)} %param.5) | copy-start | bytes 3145732
  23.1 6.8 %collective-permute-start.1 = (f32[2,2048]{1,0:T(2,128)S(1)}, f32[2,2048]{1,0:T(2,128)S(1)}, u32[]{:S(2)}, u32[]{:S(2)}) collective-permute-start(f32[2,2048]{1,0:T(2,128)S(1)} %slice.154), channel_id=1, source_target_pairs={{15,0},{0,1},{1,2},{2,3},{3,4},{4,5},{5,6},{6,7},{7,8},{8,9},{9,10... | collective-permute-start | bytes 49160 | tf_op jit(solution)/shard_map/ppermute | solution.py:12
  31.2 7.0 %collective-permute-start.2 = (f32[4,2048]{1,0:T(4,128)S(1)}, f32[4,2048]{1,0:T(4,128)S(1)}, u32[]{:S(2)}, u32[]{:S(2)}) collective-permute-start(f32[4,2048]{1,0:T(4,128)S(1)} %slice.156), channel_id=1, source_target_pairs={{15,0},{0,1},{1,2},{2,3},{3,4},{4,5},{5,6},{6,7},{7,8},{8,9},{9,10... | collective-permute-start | bytes 98312 | tf_op jit(solution)/shard_map/ppermute | solution.py:12
  39.5 7.4 %collective-permute-start.3 = (f32[8,2048]{1,0:T(8,128)S(1)}, f32[8,2048]{1,0:T(8,128)S(1)}, u32[]{:S(2)}, u32[]{:S(2)}) collective-permute-start(f32[8,2048]{1,0:T(8,128)S(1)} %slice.158), channel_id=1, source_target_pairs={{15,0},{0,1},{1,2},{2,3},{3,4},{4,5},{5,6},{6,7},{7,8},{8,9},{9,10... | collective-permute-start | bytes 196616 | tf_op jit(solution)/shard_map/ppermute | solution.py:12
  48.1 7.6 %collective-permute-start.4 = (f32[2,8,2048]{2,1,0:T(8,128)S(1)}, f32[2,8,2048]{2,1,0:T(8,128)S(1)}, u32[]{:S(2)}, u32[]{:S(2)}) collective-permute-start(f32[2,8,2048]{2,1,0:T(8,128)S(1)} %pad_maximum_fusion.4), channel_id=1, source_target_pairs={{1,0},{2,1},{3,2},{4,3},{5,4},{6,5},{7,6},{8,7},{9,8},{10,9},{11,1... | collective-permute-start | bytes 393224 | tf_op jit(solution)/shard_map/ppermute | solution.py:12
  56.1 6.2 %collective-permute-start.5 = (f32[2,4,2048]{2,1,0:T(4,128)S(1)}, f32[2,4,2048]{2,1,0:T(4,128)S(1)}, u32[]{:S(2)}, u32[]{:S(2)}) collective-permute-start(f32[2,4,2048]{2,1,0:T(4,128)S(1)} %pad_maximum_fusion.5), channel_id=1, source_target_pairs={{1,0},{2,1},{3,2},{4,3},{5,4},{6,5},{7,6},{8,7},{9,8},{10,9},{11,1... | collective-permute-start | bytes 196616 | tf_op jit(solution)/shard_map/ppermute | solution.py:12
  62.6 5.8 %collective-permute-start.6 = (f32[2,2,2048]{2,1,0:T(2,128)S(1)}, f32[2,2,2048]{2,1,0:T(2,128)S(1)}, u32[]{:S(2)}, u32[]{:S(2)}) collective-permute-start(f32[2,2,2048]{2,1,0:T(2,128)S(1)} %pad_maximum_fusion.6), channel_id=1, source_target_pairs={{1,0},{2,1},{3,2},{4,3},{5,4},{6,5},{7,6},{8,7},{9,8},{10,9},{11,1... | collective-permute-start | bytes 98312 | tf_op jit(solution)/shard_map/ppermute | solution.py:12
  68.8 6.6 %collective-permute-start.7 = (f32[2,1,2048]{2,1,0:T(1,128)S(1)}, f32[2,1,2048]{2,1,0:T(1,128)S(1)}, u32[]{:S(2)}, u32[]{:S(2)}) collective-permute-start(f32[2,1,2048]{2,1,0:T(1,128)S(1)} %pad_maximum_fusion.7), channel_id=1, source_target_pairs={{1,0},{2,1},{3,2},{4,3},{5,4},{6,5},{7,6},{8,7},{9,8},{10,9},{11,1... | collective-permute-start | bytes 49160 | tf_op jit(solution)/shard_map/ppermute | solution.py:12
  101.0 0.7 copy-start.2
  101.7 2.6 collective-permute-start.8
Sparse Core Ops, SparseCore 0:
  168.9 133.4 all-reduce.1
